TPU v7x, 512 devices: a whole 4x4x16 slice. The times are simulated.
512 devices in a mesh: band: 16 (over y, x), pix: 32 (over z, core).
Axes of the slice: x: 4, y: 4, z: 16, core: 2. Of those that a mesh axis runs over, the one named last changes fastest.
Arguments:
- pixels: bfloat16 [512, 32, 1024], P('pix', 'band'), may hold values from -6 to 6
- clear_count: int32 [32], P('pix'), may hold values from 3 to 10, as said below
- clear_index: int32 [320], P('pix'), may hold values from 0 to 15, as said below
- attn_gain: float32 [1024], replicated, may hold values from 0.1 to 1.9
- w_query: bfloat16 [1024, 1024], P(None, 'band')
- w_key: bfloat16 [1024, 1024], P(None, 'band')
- w_value: bfloat16 [1024, 1024], P(None, 'band'), may hold values from -0.1875 to 0.1875
- w_out: bfloat16 [1024, 1024], P('band'), may hold values from -0.1875 to 0.1875
- mlp_gain: float32 [1024], replicated, may hold values from 0.1 to 1.9
- w_gate: bfloat16 [1024, 4096], P(None, 'band'), may hold values from -0.1875 to 0.1875
- w_up: bfloat16 [1024, 4096], P(None, 'band'), may hold values from -0.1875 to 0.1875
- w_down: bfloat16 [4096, 1024], P('band'), may hold values from -0.09375 to 0.09375
Outputs:
- updated: bfloat16 [512, 32, 1024], P('pix', 'band')
Inputs may be any that keep to these rules, and one draw needn't show every extreme that they name: `clear_count`: some tile, drawn from the seed, keeps exactly 10 clear pixels. `clear_index`: for tile t, entries t*10 to t*10+clear_count[t]-1 are distinct local pixel indices in rising order; the tile's remaining entries are 0.
All inputs are finite; a program needn't handle non-finite values.
Results may differ from a plain program's by a relative error of at most 0.019.
Values may be sent and summed in bfloat16 or wider, within the bound.
No kernel may reach another device: no remote copies, remote signals or barrier semaphores. Data moves between devices by JAX's collectives and lax.ppermute only.
A program may use at most 64 MiB of HBM per device.

v0:
```python
import jax
import jax.numpy as jnp
from jax import lax
from jax.sharding import PartitionSpec as P

HD = 64


def normed(rows, gain):
    full = rows.astype(jnp.float32)
    scaled = full * lax.rsqrt(jnp.mean(full * full, axis=-1, keepdims=True) + 1e-05)
    return (scaled * gain).astype(jnp.bfloat16)


def slot_live(number, slots_per_tile, counts):
    slot = jnp.arange(number, dtype=jnp.int32)
    owner = slot // slots_per_tile
    owned = owner[:, None] == jnp.arange(counts.shape[0], dtype=jnp.int32)[None, :]
    owner_count = jnp.sum(jnp.where(owned, counts[None, :], 0), axis=1)
    return slot % slots_per_tile < owner_count


def shards(
    pixels,
    clear_count,
    clear_index,
    attn_gain,
    w_query,
    w_key,
    w_value,
    w_out,
    mlp_gain,
    w_gate,
    w_up,
    w_down,
):
    own_count = clear_count[0]
    kept = jnp.take(pixels, clear_index, axis=0)
    kept_rows = jnp.swapaxes(kept, 0, 1)
    all_rows = lax.all_gather(kept_rows, "band", axis=0, tiled=True)
    spec, slots_here, width = all_rows.shape
    heads_here = w_query.shape[1] // HD
    flat = normed(all_rows, attn_gain).reshape(spec * slots_here, width)

    def project(weight):
        out = jnp.dot(flat, weight, preferred_element_type=jnp.float32).astype(jnp.bfloat16)
        return out.reshape(spec, slots_here, heads_here, HD)

    query = project(w_query)
    key = project(w_key)
    value = project(w_value)
    counts = lax.all_gather(clear_count, "pix", axis=0, tiled=True)
    start_top = jnp.full((spec, heads_here, slots_here), -1e30, jnp.float32)
    top = start_top
    key_piece = lax.all_gather(key, "pix", axis=1, tiled=True)
    value_piece = lax.all_gather(value, "pix", axis=1, tiled=True)
    live = slot_live(key_piece.shape[1], slots_here, counts)
    scores = jnp.einsum(
        "sqhd,skhd->shqk", query, key_piece, preferred_element_type=jnp.float32
    ) * HD ** (-0.5)
    masked = jnp.where(live[None, None, None, :], scores, -1e30)
    new_top = jnp.maximum(top, jnp.max(masked, axis=-1))
    expo = jnp.where(live[None, None, None, :], jnp.exp(masked - new_top[..., None]), 0.0)
    totals = jnp.sum(expo, axis=-1)
    mixed = jnp.einsum(
        "shqk,skhd->sqhd",
        expo.astype(jnp.bfloat16),
        value_piece,
        preferred_element_type=jnp.float32,
    )
    acc = mixed
    top, totals, acc = (new_top, totals, acc)
    context = (acc / jnp.transpose(totals, (0, 2, 1))[..., None]).astype(jnp.bfloat16)
    context_rows = context.reshape(spec, slots_here, heads_here * HD)
    spec_here = spec // lax.axis_size("band")
    piece = context_rows
    out = jnp.dot(
        piece.reshape(spec_here * lax.axis_size("band") * slots_here, heads_here * HD),
        w_out,
        preferred_element_type=jnp.float32,
    )
    attn_out = lax.psum_scatter(
        out.reshape(spec_here * lax.axis_size("band"), slots_here, width).astype(jnp.bfloat16),
        "band",
        scatter_dimension=0,
        tiled=True,
    ).astype(jnp.float32)
    state = (kept_rows.astype(jnp.float32) + attn_out).astype(jnp.bfloat16)
    mlp_in = lax.all_gather(normed(state, mlp_gain), "band", axis=0, tiled=True)
    piece = mlp_in.reshape(spec_here * lax.axis_size("band") * slots_here, width)
    gate = jnp.dot(piece, w_gate, preferred_element_type=jnp.float32)
    upper = jnp.dot(piece, w_up, preferred_element_type=jnp.float32)
    hidden = (jax.nn.silu(gate) * upper).astype(jnp.bfloat16)
    out = jnp.dot(hidden, w_down, preferred_element_type=jnp.float32)
    mlp_out = lax.psum_scatter(
        out.reshape(spec_here * lax.axis_size("band"), slots_here, width).astype(jnp.bfloat16),
        "band",
        scatter_dimension=0,
        tiled=True,
    ).astype(jnp.float32)
    encoded = (state.astype(jnp.float32) + mlp_out).astype(jnp.bfloat16)
    live_here = jnp.arange(slots_here, dtype=jnp.int32) < own_count
    chosen = (
        jnp.arange(pixels.shape[0], dtype=jnp.int32)[:, None] == clear_index[None, :]
    ) & live_here[None, :]
    placed = jnp.einsum(
        "pc,scd->psd", chosen.astype(jnp.bfloat16), encoded, preferred_element_type=jnp.float32
    ).astype(jnp.bfloat16)
    taken = jnp.any(chosen, axis=1)
    return jnp.where(taken[:, None, None], placed, pixels)


def solution(mesh):
    return jax.shard_map(
        shards,
        mesh=mesh,
        in_specs=(
            P("pix", "band", None),
            P("pix"),
            P("pix"),
            P(),
            P(None, "band"),
            P(None, "band"),
            P(None, "band"),
            P("band", None),
            P(),
            P(None, "band"),
            P(None, "band"),
            P("band", None),
        ),
        out_specs=P("pix", "band", None),
        check_vma=False,
    )
```

profile of v0, /device:TPU:2, one launch (start us, length us, event | category | flops | bytes accessed | tf_op | source)
XLA Modules:
  0.0 454.2 jit_solution(5196698798898972980)
XLA Ops:
  6.5 0.7 compare_select_fusion
  7.3 0.7 compare_and_fusion
  7.9 1.5 gather_fusion
  9.4 0.1 fusion.46
  9.6 27.7 %all_gather.15 = bf16[32,10,1024]{2,1,0:T(8,128)(2,1)S(1)} all-gather(bf16[2,10,1024]{2,1,0:T(8,128)(2,1)S(1)} %copy.59), channel_id=1, replica_groups=mesh['band'=16,'pix'=32] {'band'}, dimensions={0}, use_global_device_ids=true | all-gather | bytes 696320 | tf_op jit(solution)/shard_map/all_gather | solution.py:40
  37.3 0.3 fusion
  37.6 0.3 fusion.2
  37.9 0.2 reshape.109
  38.2 0.3 copy-done.2
  38.5 0.3 convolution_convert_fusion.3
  38.9 0.1 copy.64
  39.0 0.7 copy.65
  39.7 0.0 all-gather.3.cloned.1.call-start
  39.8 0.3 convolution_convert_fusion.5
  40.1 0.1 copy.60
  40.3 0.7 copy.61
  41.0 0.0 all-reduce.6.cloned.1.call-start
  41.1 0.3 convolution_convert_fusion.4
  41.4 0.1 copy.63
  42.2 1.3 dynamic-slice
  43.5 0.7 dynamic-update-slice
  44.2 24.1 %all-reduce = s32[32]{0:T(128)S(1)} all-reduce(s32[32]{0:T(128)S(1)} %dynamic-update-slice), channel_id=1, replica_groups=mesh['band'=16,'pix'=32] {'pix'}, use_global_device_ids=true, to_apply=%add | all-reduce | flops 32 | bytes 256
  68.3 0.1 select_reduce_fusion
  68.4 43.2 %all-gather.5.cloned.1.call-done = bf16[32,320,1,64]{3,0,2,1:T(8,128)(2,1)} async-done(((bf16[32,10,1,64]{3,0,2,1:T(8,128)(2,1)}), bf16[32,320,1,64]{3,0,2,1:T(8,128)(2,1)}) %all-gather.5.cloned.1.call-update) | async-done | bytes 1310736 | tf_op jit(solution)/shard_map/all_gather | solution.py:55
  111.6 4.4 copy.66
  116.0 0.5 fusion.61
  116.5 0.3 fusion.27
  116.8 65.8 %all-gather.3.cloned.1.call-done = bf16[32,320,1,64]{3,0,2,1:T(8,128)(2,1)} async-done(((bf16[32,10,1,64]{3,0,2,1:T(8,128)(2,1)}), bf16[32,320,1,64]{3,0,2,1:T(8,128)(2,1)}) %all-gather.3.cloned.1.call-update) | async-done | bytes 1310736 | tf_op jit(solution)/shard_map/all_gather | solution.py:56
  182.7 4.4 copy.62
  187.1 0.7 fusion.24
  187.8 0.2 copy-done.5
  188.0 1.2 convolution_convert_fusion
  189.3 1.3 dynamic-slice.1
  191.2 110.8 %all-reduce.6.cloned.1.call-done = bf16[32,10,1024]{2,0,1:T(8,128)(2,1)} async-done(((bf16[32,10,1024]{2,0,1:T(8,128)(2,1)}), bf16[32,10,1024]{2,0,1:T(8,128)(2,1)}) %all-reduce.6.cloned.1.call-update) | async-done | bytes 655376
  302.0 1.1 fusion.40
  303.2 0.1 fusion.42
  303.3 23.2 %all_gather.19 = bf16[32,10,1024]{2,1,0:T(8,128)(2,1)S(1)} all-gather(bf16[2,10,1024]{2,1,0:T(8,128)(2,1)S(1)} %copy.68), channel_id=1, replica_groups=mesh['band'=16,'pix'=32] {'band'}, dimensions={0}, use_global_device_ids=true | all-gather | bytes 696320 | tf_op jit(solution)/shard_map/all_gather | solution.py:89
  326.5 0.2 reshape.115
  326.8 0.3 fusion.62
  327.1 0.4 copy-done.9
  327.6 0.9 convolution_convert_fusion.1
  328.4 0.2 convert_element_type.79
  328.7 1.2 copy.69
  329.9 0.1 fusion.49
  330.0 115.7 %all-reduce.8.cloned.1.call-done = bf16[32,10,1024]{2,0,1:T(8,128)(2,1)} async-done(((bf16[32,10,1024]{2,0,1:T(8,128)(2,1)}), bf16[32,10,1024]{2,0,1:T(8,128)(2,1)}) %all-reduce.8.cloned.1.call-update) | async-done | bytes 655376
  445.8 1.0 fusion.43
  446.8 0.1 fusion.17
  446.9 0.7 copy.72
  (38 shorter events, 0.4 us)
Async XLA Ops:
  6.5 320.6 %copy-start = (bf16[256,1024]{1,0:T(8,128)(2,1)S(1)}, bf16[256,1024]{1,0:T(8,128)(2,1)}, u32[]{:S(2)}) copy-start(bf16[256,1024]{1,0:T(8,128)(2,1)} %param.23) | copy-start | bytes 1572868
  6.5 31.1 %copy-start.7 = (f32[1024]{0:T(1024)S(1)}, f32[1024]{0:T(1024)}, u32[]{:S(2)}) copy-start(f32[1024]{0:T(1024)} %param.15) | copy-start | bytes 12292
  6.5 105.1 %all-gather.5.cloned.1.call-start = ((), (), s32[]{:S(2)}) async-start(), calls=%async_computation.1 | async-start | bytes 2703360 | tf_op jit(solution)/shard_map/all_gather | solution.py:55
  37.6 0.9 copy-start.2
  37.9 1.8 copy-start.3
  38.5 2.5 copy-start.4
  39.7 142.9 %all-gather.3.cloned.1.call-start = ((), (), s32[]{:S(2)}) async-start(), calls=%async_computation | async-start | bytes 2703360 | tf_op jit(solution)/shard_map/all_gather | solution.py:56
  41.0 261.0 %all-reduce.6.cloned.1.call-start = ((), (), s32[]{:S(2)}) async-start(), calls=%async_computation.2 | async-start | bytes 1310720
  187.1 0.9 copy-start.5
  188.0 115.2 %copy-start.8 = (f32[1024]{0:T(1024)S(1)}, f32[1024]{0:T(1024)}, u32[]{:S(2)}) copy-start(f32[1024]{0:T(1024)} %param.20) | copy-start | bytes 12292
  189.2 256.6 %all-reduce.8.cloned.1.call-start = ((), (), s32[]{:S(2)}) async-start(), calls=%async_computation.3 | async-start | bytes 1310720
  191.2 135.5 %copy-start.1 = (bf16[1024,256]{1,0:T(8,128)(2,1)S(1)}, bf16[1024,256]{1,0:T(8,128)(2,1)}, u32[]{:S(2)}) copy-start(bf16[1024,256]{1,0:T(8,128)(2,1)} %param.21) | copy-start | bytes 1572868
  326.5 1.0 copy-start.9
  328.6 1.3 copy-start.10
  328.6 118.1 %copy-start.6 = (bf16[16,2,1024]{2,1,0:T(2,128)(2,1)S(1)}, bf16[16,2,1024]{2,1,0:T(2,128)(2,1)}, u32[]{:S(2)}) copy-start(bf16[16,2,1024]{2,1,0:T(2,128)(2,1)} %param.12) | copy-start | bytes 196612
Sparse Core Ops, SparseCore 0:
  39.8 71.7 all-gather.4
  113.7 68.9 all-gather.2
  189.3 112.6 all-reduce.5
  330.0 115.7 all-reduce.7
where the time goes:
time: 455 us; the launch traced here: 454 us
  waiting for transfers between devices  336 us (74%)
  blocking collectives  75 us (16%)
  local copies, waits for them, and re-layouts  19 us (4%)
  between operations  14.7 us (3%)
  other arithmetic  4.92 us (1%)
  matrix products  4.72 us (1%)
    unnamed x6, waiting for transfers between devices  227 us
    all_gather x1, waiting for transfers between devices, shards(): value_piece = lax.all_gather(value, 'pix', axis=1, tiled=True)  65.8 us
    all_gather x1, waiting for transfers between devices, shards(): key_piece = lax.all_gather(key, 'pix', axis=1, tiled=True)  43.2 us
    all_gather x1, blocking collectives, shards(): all_rows = lax.all_gather(kept_rows, 'band', axis=0, tiled=True)  27.7 us
    unnamed x1, blocking collectives  24.1 us
    all_gather x1, blocking collectives, shards(): mlp_in = lax.all_gather(normed(state, mlp_gain), 'band', axis=0, tiled=True)  23.2 us
  transfers between devices with their start and end apart: 4, of which 4 were waited for; matrix products, arithmetic and copies ran while one was open for 2% of the time, Pallas kernels for 0%

commit v1 on v0

--- a/solution.py
+++ b/solution.py
@@ -86,7 +86,26 @@
         tiled=True,
     ).astype(jnp.float32)
     state = (kept_rows.astype(jnp.float32) + attn_out).astype(jnp.bfloat16)
-    mlp_in = lax.all_gather(normed(state, mlp_gain), "band", axis=0, tiled=True)
+    array = normed(state, mlp_gain)
+    ways, here, step = (lax.axis_size("band"), lax.axis_index("band"), array.shape[0])
+    dims = [n * ways if d == 0 else n for d, n in enumerate(array.shape)]
+    full_2 = lax.dynamic_update_slice_in_dim(
+        jnp.zeros(dims, array.dtype), array, here * step, axis=0
+    )
+    going_up = going_down = array
+    for far in range(1, ways // 2 + 1):
+        going_up = lax.ppermute(going_up, "band", [(d, (d + 1) % ways) for d in range(ways)])
+        full_2 = lax.dynamic_update_slice_in_dim(
+            full_2, going_up, (here - far) % ways * step, axis=0
+        )
+        if 2 * far < ways:
+            going_down = lax.ppermute(
+                going_down, "band", [(d, (d - 1) % ways) for d in range(ways)]
+            )
+            full_2 = lax.dynamic_update_slice_in_dim(
+                full_2, going_down, (here + far) % ways * step, axis=0
+            )
+    mlp_in = full_2
     piece = mlp_in.reshape(spec_here * lax.axis_size("band") * slots_here, width)
     gate = jnp.dot(piece, w_gate, preferred_element_type=jnp.float32)
     upper = jnp.dot(piece, w_up, preferred_element_type=jnp.float32)

time: 455 us -> 503 us (1.11)
  starting transfers between devices: 0.13 us -> 61.9 us
  blocking collectives: 75 us -> 51.9 us
  waiting for transfers between devices: 336 us -> 344 us
    ppermute x0 -> x15, starting transfers between devices: none -> 61.7 us  [the longest x7 44.6 us: shards(): lax.ppermute(going_down, 'band', [(d, (d - 1) % ways) for d in range(ways)])]
    all_gather x1 -> x0, blocking collectives: 23.2 us -> none  [shards(): mlp_in = lax.all_gather(normed(state, mlp_gain), 'band', axis=0, tiled=True)]
    ppermute x0 -> x15, waiting for transfers between devices: none -> 7.27 us  [the longest x8 7.25 us: shards(): lax.ppermute(going_up, 'band', [(d, (d + 1) % ways) for d in range(ways)])]
  transfers between devices with their start and end apart: 4 -> 19, of which waited for: 4 -> 5; matrix products, arithmetic and copies ran while one was open for 2% -> 2% of each run, Pallas kernels for 0% -> 0%
where the time goes in v1:
time: 503 us
  waiting for transfers between devices  344 us (68%)
  starting transfers between devices  61.9 us (12%)
  blocking collectives  51.9 us (10%)
  local copies, waits for them, and re-layouts  19 us (4%)
  between operations  15.4 us (3%)
  matrix products  5.77 us (1%)
    unnamed x6, waiting for transfers between devices  228 us
    all_gather x1, waiting for transfers between devices, shards(): value_piece = lax.all_gather(value, 'pix', axis=1, tiled=True)  65.8 us
    ppermute x7, starting transfers between devices, shards(): lax.ppermute(going_down, 'band', [(d, (d - 1) % ways) for d in range(ways)])  44.6 us
    all_gather x1, waiting for transfers between devices, shards(): key_piece = lax.all_gather(key, 'pix', axis=1, tiled=True)  43 us
    all_gather x1, blocking collectives, shards(): all_rows = lax.all_gather(kept_rows, 'band', axis=0, tiled=True)  27.7 us
    unnamed x1, blocking collectives  24.2 us
    ppermute x8, starting transfers between devices, shards(): lax.ppermute(going_up, 'band', [(d, (d + 1) % ways) for d in range(ways)])  17.1 us
  transfers between devices with their start and end apart: 19, of which 5 were waited for; matrix products, arithmetic and copies ran while one was open for 2% of the time, Pallas kernels for 0%

profile of v1, /device:TPU:2, one launch (start us, length us, event | category | flops | bytes accessed | tf_op | source)
XLA Modules:
  0.0 502.6 jit_solution(18332661027966979130)
XLA Ops:
  6.5 0.7 compare_select_fusion
  7.3 0.7 compare_and_fusion
  7.9 1.5 gather_fusion
  9.6 27.7 %all_gather.12 = bf16[32,10,1024]{2,1,0:T(8,128)(2,1)S(1)} all-gather(bf16[2,10,1024]{2,1,0:T(8,128)(2,1)S(1)} %copy.89), channel_id=1, replica_groups=mesh['band'=16,'pix'=32] {'band'}, dimensions={0}, use_global_device_ids=true | all-gather | bytes 696320 | tf_op jit(solution)/shard_map/all_gather | solution.py:40
  37.3 0.3 fusion
  37.6 0.3 fusion.2
  38.2 0.3 copy-done.2
  38.5 0.3 convolution_convert_fusion.3
  39.0 0.7 copy.95
  39.8 0.3 convolution_convert_fusion.5
  40.3 0.7 copy.91
  41.1 0.3 convolution_convert_fusion.4
  42.2 1.3 dynamic-slice
  43.5 0.7 dynamic-update-slice
  44.3 24.2 %all-reduce = s32[32]{0:T(128)S(1)} all-reduce(s32[32]{0:T(128)S(1)} %dynamic-update-slice), channel_id=1, replica_groups=mesh['band'=16,'pix'=32] {'pix'}, use_global_device_ids=true, to_apply=%add | all-reduce | flops 32 | bytes 256
  68.5 43.0 %all-gather.5.cloned.1.call-done = bf16[32,320,1,64]{3,0,2,1:T(8,128)(2,1)} async-done(((bf16[32,10,1,64]{3,0,2,1:T(8,128)(2,1)}), bf16[32,320,1,64]{3,0,2,1:T(8,128)(2,1)}) %all-gather.5.cloned.1.call-update) | async-done | bytes 1310736 | tf_op jit(solution)/shard_map/all_gather | solution.py:55
  111.6 4.4 copy.96
  116.0 0.5 fusion.55
  116.5 0.3 fusion.26
  116.8 65.8 %all-gather.3.cloned.1.call-done = bf16[32,320,1,64]{3,0,2,1:T(8,128)(2,1)} async-done(((bf16[32,10,1,64]{3,0,2,1:T(8,128)(2,1)}), bf16[32,320,1,64]{3,0,2,1:T(8,128)(2,1)}) %all-gather.3.cloned.1.call-update) | async-done | bytes 1310736 | tf_op jit(solution)/shard_map/all_gather | solution.py:56
  182.6 4.4 copy.92
  187.1 0.7 fusion.23
  188.0 1.2 convolution_convert_fusion
  189.5 1.3 dynamic-slice.1
  191.5 110.5 %all-reduce.6.cloned.1.call-done = bf16[32,10,1024]{2,0,1:T(8,128)(2,1)} async-done(((bf16[32,10,1024]{2,0,1:T(8,128)(2,1)}), bf16[32,10,1024]{2,0,1:T(8,128)(2,1)}) %all-reduce.6.cloned.1.call-update) | async-done | bytes 655376
  302.0 1.1 fusion.34
  303.3 2.7 collective-permute-start
  306.0 3.1 collective-permute-start.1
  309.3 2.7 collective-permute-start.2
  312.0 5.3 %collective-permute-start.3 = (bf16[2,10,1024]{2,0,1:T(2,128)(2,1)S(1)}, bf16[2,10,1024]{2,0,1:T(2,128)(2,1)S(1)}, u32[]{:S(2)}, u32[]{:S(2)}) collective-permute-start(bf16[2,10,1024]{2,0,1:T(2,128)(2,1)S(1)} %collective-permute-done.1), channel_id=1, source_target_pairs={{0,480},{32,0},{64,32},{96,64},{128,96},{160,128},{192,160},{224,1... | collective-permute-start | bytes 122888 | tf_op jit(solution)/shard_map/ppermute | solution.py:102
  317.4 2.1 collective-permute-start.4
  319.5 7.2 %collective-permute-start.5 = (bf16[2,10,1024]{2,0,1:T(2,128)(2,1)S(1)}, bf16[2,10,1024]{2,0,1:T(2,128)(2,1)S(1)}, u32[]{:S(2)}, u32[]{:S(2)}) collective-permute-start(bf16[2,10,1024]{2,0,1:T(2,128)(2,1)S(1)} %collective-permute-done.3), channel_id=1, source_target_pairs={{0,480},{32,0},{64,32},{96,64},{128,96},{160,128},{192,160},{224,1... | collective-permute-start | bytes 122888 | tf_op jit(solution)/shard_map/ppermute | solution.py:102
  326.8 1.9 collective-permute-start.6
  328.7 7.2 %collective-permute-start.7 = (bf16[2,10,1024]{2,0,1:T(2,128)(2,1)S(1)}, bf16[2,10,1024]{2,0,1:T(2,128)(2,1)S(1)}, u32[]{:S(2)}, u32[]{:S(2)}) collective-permute-start(bf16[2,10,1024]{2,0,1:T(2,128)(2,1)S(1)} %collective-permute-done.5), channel_id=1, source_target_pairs={{0,480},{32,0},{64,32},{96,64},{128,96},{160,128},{192,160},{224,1... | collective-permute-start | bytes 122888 | tf_op jit(solution)/shard_map/ppermute | solution.py:102
  336.0 1.9 collective-permute-start.8
  338.0 7.2 %collective-permute-start.9 = (bf16[2,10,1024]{2,0,1:T(2,128)(2,1)S(1)}, bf16[2,10,1024]{2,0,1:T(2,128)(2,1)S(1)}, u32[]{:S(2)}, u32[]{:S(2)}) collective-permute-start(bf16[2,10,1024]{2,0,1:T(2,128)(2,1)S(1)} %collective-permute-done.7), channel_id=1, source_target_pairs={{0,480},{32,0},{64,32},{96,64},{128,96},{160,128},{192,160},{224,1... | collective-permute-start | bytes 122888 | tf_op jit(solution)/shard_map/ppermute | solution.py:102
  345.3 1.9 collective-permute-start.10
  347.2 7.2 %collective-permute-start.11 = (bf16[2,10,1024]{2,0,1:T(2,128)(2,1)S(1)}, bf16[2,10,1024]{2,0,1:T(2,128)(2,1)S(1)}, u32[]{:S(2)}, u32[]{:S(2)}) collective-permute-start(bf16[2,10,1024]{2,0,1:T(2,128)(2,1)S(1)} %collective-permute-done.9), channel_id=1, source_target_pairs={{0,480},{32,0},{64,32},{96,64},{128,96},{160,128},{192,160},{224,1... | collective-permute-start | bytes 122888 | tf_op jit(solution)/shard_map/ppermute | solution.py:102
  354.5 1.9 collective-permute-start.12
  356.5 7.2 %collective-permute-start.13 = (bf16[2,10,1024]{2,0,1:T(2,128)(2,1)S(1)}, bf16[2,10,1024]{2,0,1:T(2,128)(2,1)S(1)}, u32[]{:S(2)}, u32[]{:S(2)}) collective-permute-start(bf16[2,10,1024]{2,0,1:T(2,128)(2,1)S(1)} %collective-permute-done.11), channel_id=1, source_target_pairs={{0,480},{32,0},{64,32},{96,64},{128,96},{160,128},{192,160},{224,1... | collective-permute-start | bytes 122888 | tf_op jit(solution)/shard_map/ppermute | solution.py:102
  363.8 1.9 collective-permute-start.14
  365.8 7.2 %collective-permute-done.14 = bf16[2,10,1024]{2,0,1:T(2,128)(2,1)S(1)} collective-permute-done((bf16[2,10,1024]{2,0,1:T(2,128)(2,1)S(1)}, bf16[2,10,1024]{2,0,1:T(2,128)(2,1)S(1)}, u32[]{:S(2)}, u32[]{:S(2)}) %collective-permute-start.14) | collective-permute-done | bytes 40992 | tf_op jit(solution)/shard_map/ppermute | solution.py:97
  373.3 0.3 fusion.58
  373.6 1.9 convolution_convert_fusion.1
  375.8 1.2 copy.114
  377.2 117.1 %all-reduce.8.cloned.1.call-done = bf16[32,10,1024]{2,0,1:T(8,128)(2,1)} async-done(((bf16[32,10,1024]{2,0,1:T(8,128)(2,1)}), bf16[32,10,1024]{2,0,1:T(8,128)(2,1)}) %all-reduce.8.cloned.1.call-update) | async-done | bytes 655376
  494.2 1.0 fusion.37
  495.4 0.7 copy.117
  (81 shorter events, 2.6 us)
Async XLA Ops:
  6.5 367.1 %copy-start = (bf16[256,1024]{1,0:T(8,128)(2,1)S(1)}, bf16[256,1024]{1,0:T(8,128)(2,1)}, u32[]{:S(2)}) copy-start(bf16[256,1024]{1,0:T(8,128)(2,1)} %param.23) | copy-start | bytes 1572868
  6.5 31.1 %copy-start.7 = (f32[1024]{0:T(1024)S(1)}, f32[1024]{0:T(1024)}, u32[]{:S(2)}) copy-start(f32[1024]{0:T(1024)} %param.15) | copy-start | bytes 12292
  6.5 105.0 %all-gather.5.cloned.1.call-start = ((), (), s32[]{:S(2)}) async-start(), calls=%async_computation.1 | async-start | bytes 2703360 | tf_op jit(solution)/shard_map/all_gather | solution.py:55
  37.6 0.9 copy-start.2
  37.9 1.9 copy-start.3
  38.5 2.5 copy-start.4
  39.7 142.9 %all-gather.3.cloned.1.call-start = ((), (), s32[]{:S(2)}) async-start(), calls=%async_computation | async-start | bytes 2703360 | tf_op jit(solution)/shard_map/all_gather | solution.py:56
  41.0 261.0 %all-reduce.6.cloned.1.call-start = ((), (), s32[]{:S(2)}) async-start(), calls=%async_computation.2 | async-start | bytes 1310720
  187.1 0.9 copy-start.5
  188.0 115.2 %copy-start.8 = (f32[1024]{0:T(1024)S(1)}, f32[1024]{0:T(1024)}, u32[]{:S(2)}) copy-start(f32[1024]{0:T(1024)} %param.20) | copy-start | bytes 12292
  189.2 305.0 %all-reduce.8.cloned.1.call-start = ((), (), s32[]{:S(2)}) async-start(), calls=%async_computation.3 | async-start | bytes 1310720
  303.3 6.0 %collective-permute-start = (bf16[2,10,1024]{2,0,1:T(2,128)(2,1)S(1)}, bf16[2,10,1024]{2,0,1:T(2,128)(2,1)S(1)}, u32[]{:S(2)}, u32[]{:S(2)}) collective-permute-start(bf16[2,10,1024]{2,0,1:T(2,128)(2,1)S(1)} %fusion.36), channel_id=1, source_target_pairs={{0,32},{32,64},{64,96},{96,128},{128,160},{160,192},{192,224},{224... | collective-permute-start | bytes 122888 | tf_op jit(solution)/shard_map/ppermute | solution.py:97
  306.0 6.0 %collective-permute-start.1 = (bf16[2,10,1024]{2,0,1:T(2,128)(2,1)S(1)}, bf16[2,10,1024]{2,0,1:T(2,128)(2,1)S(1)}, u32[]{:S(2)}, u32[]{:S(2)}) collective-permute-start(bf16[2,10,1024]{2,0,1:T(2,128)(2,1)S(1)} %fusion.36), channel_id=1, source_target_pairs={{0,480},{32,0},{64,32},{96,64},{128,96},{160,128},{192,160},{224,1... | collective-permute-start | bytes 122888 | tf_op jit(solution)/shard_map/ppermute | solution.py:102
  309.3 8.1 %collective-permute-start.2 = (bf16[2,10,1024]{2,0,1:T(2,128)(2,1)S(1)}, bf16[2,10,1024]{2,0,1:T(2,128)(2,1)S(1)}, u32[]{:S(2)}, u32[]{:S(2)}) collective-permute-start(bf16[2,10,1024]{2,0,1:T(2,128)(2,1)S(1)} %collective-permute-done), channel_id=1, source_target_pairs={{0,32},{32,64},{64,96},{96,128},{128,160},{160,192},{192,224},{224... | collective-permute-start | bytes 122888 | tf_op jit(solution)/shard_map/ppermute | solution.py:97
  312.0 7.4 %collective-permute-start.3 = (bf16[2,10,1024]{2,0,1:T(2,128)(2,1)S(1)}, bf16[2,10,1024]{2,0,1:T(2,128)(2,1)S(1)}, u32[]{:S(2)}, u32[]{:S(2)}) collective-permute-start(bf16[2,10,1024]{2,0,1:T(2,128)(2,1)S(1)} %collective-permute-done.1), channel_id=1, source_target_pairs={{0,480},{32,0},{64,32},{96,64},{128,96},{160,128},{192,160},{224,1... | collective-permute-start | bytes 122888 | tf_op jit(solution)/shard_map/ppermute | solution.py:102
  317.4 55.9 %copy-start.1 = (bf16[1024,256]{1,0:T(8,128)(2,1)S(1)}, bf16[1024,256]{1,0:T(8,128)(2,1)}, u32[]{:S(2)}) copy-start(bf16[1024,256]{1,0:T(8,128)(2,1)} %param.21) | copy-start | bytes 1572868
  317.4 9.4 %collective-permute-start.4 = (bf16[2,10,1024]{2,0,1:T(2,128)(2,1)S(1)}, bf16[2,10,1024]{2,0,1:T(2,128)(2,1)S(1)}, u32[]{:S(2)}, u32[]{:S(2)}) collective-permute-start(bf16[2,10,1024]{2,0,1:T(2,128)(2,1)S(1)} %collective-permute-done.2), channel_id=1, source_target_pairs={{0,32},{32,64},{64,96},{96,128},{128,160},{160,192},{192,224},{224... | collective-permute-start | bytes 122888 | tf_op jit(solution)/shard_map/ppermute | solution.py:97
  319.5 9.2 %collective-permute-start.5 = (bf16[2,10,1024]{2,0,1:T(2,128)(2,1)S(1)}, bf16[2,10,1024]{2,0,1:T(2,128)(2,1)S(1)}, u32[]{:S(2)}, u32[]{:S(2)}) collective-permute-start(bf16[2,10,1024]{2,0,1:T(2,128)(2,1)S(1)} %collective-permute-done.3), channel_id=1, source_target_pairs={{0,480},{32,0},{64,32},{96,64},{128,96},{160,128},{192,160},{224,1... | collective-permute-start | bytes 122888 | tf_op jit(solution)/shard_map/ppermute | solution.py:102
  326.8 9.2 %collective-permute-start.6 = (bf16[2,10,1024]{2,0,1:T(2,128)(2,1)S(1)}, bf16[2,10,1024]{2,0,1:T(2,128)(2,1)S(1)}, u32[]{:S(2)}, u32[]{:S(2)}) collective-permute-start(bf16[2,10,1024]{2,0,1:T(2,128)(2,1)S(1)} %collective-permute-done.4), channel_id=1, source_target_pairs={{0,32},{32,64},{64,96},{96,128},{128,160},{160,192},{192,224},{224... | collective-permute-start | bytes 122888 | tf_op jit(solution)/shard_map/ppermute | solution.py:97
  328.7 9.2 %collective-permute-start.7 = (bf16[2,10,1024]{2,0,1:T(2,128)(2,1)S(1)}, bf16[2,10,1024]{2,0,1:T(2,128)(2,1)S(1)}, u32[]{:S(2)}, u32[]{:S(2)}) collective-permute-start(bf16[2,10,1024]{2,0,1:T(2,128)(2,1)S(1)} %collective-permute-done.5), channel_id=1, source_target_pairs={{0,480},{32,0},{64,32},{96,64},{128,96},{160,128},{192,160},{224,1... | collective-permute-start | bytes 122888 | tf_op jit(solution)/shard_map/ppermute | solution.py:102
  336.0 9.2 %collective-permute-start.8 = (bf16[2,10,1024]{2,0,1:T(2,128)(2,1)S(1)}, bf16[2,10,1024]{2,0,1:T(2,128)(2,1)S(1)}, u32[]{:S(2)}, u32[]{:S(2)}) collective-permute-start(bf16[2,10,1024]{2,0,1:T(2,128)(2,1)S(1)} %collective-permute-done.6), channel_id=1, source_target_pairs={{0,32},{32,64},{64,96},{96,128},{128,160},{160,192},{192,224},{224... | collective-permute-start | bytes 122888 | tf_op jit(solution)/shard_map/ppermute | solution.py:97
  338.0 9.2 %collective-permute-start.9 = (bf16[2,10,1024]{2,0,1:T(2,128)(2,1)S(1)}, bf16[2,10,1024]{2,0,1:T(2,128)(2,1)S(1)}, u32[]{:S(2)}, u32[]{:S(2)}) collective-permute-start(bf16[2,10,1024]{2,0,1:T(2,128)(2,1)S(1)} %collective-permute-done.7), channel_id=1, source_target_pairs={{0,480},{32,0},{64,32},{96,64},{128,96},{160,128},{192,160},{224,1... | collective-permute-start | bytes 122888 | tf_op jit(solution)/shard_map/ppermute | solution.py:102
  345.3 9.2 %collective-permute-start.10 = (bf16[2,10,1024]{2,0,1:T(2,128)(2,1)S(1)}, bf16[2,10,1024]{2,0,1:T(2,128)(2,1)S(1)}, u32[]{:S(2)}, u32[]{:S(2)}) collective-permute-start(bf16[2,10,1024]{2,0,1:T(2,128)(2,1)S(1)} %collective-permute-done.8), channel_id=1, source_target_pairs={{0,32},{32,64},{64,96},{96,128},{128,160},{160,192},{192,224},{224... | collective-permute-start | bytes 122888 | tf_op jit(solution)/shard_map/ppermute | solution.py:97
  347.2 9.2 %collective-permute-start.11 = (bf16[2,10,1024]{2,0,1:T(2,128)(2,1)S(1)}, bf16[2,10,1024]{2,0,1:T(2,128)(2,1)S(1)}, u32[]{:S(2)}, u32[]{:S(2)}) collective-permute-start(bf16[2,10,1024]{2,0,1:T(2,128)(2,1)S(1)} %collective-permute-done.9), channel_id=1, source_target_pairs={{0,480},{32,0},{64,32},{96,64},{128,96},{160,128},{192,160},{224,1... | collective-permute-start | bytes 122888 | tf_op jit(solution)/shard_map/ppermute | solution.py:102
  354.5 9.2 %collective-permute-start.12 = (bf16[2,10,1024]{2,0,1:T(2,128)(2,1)S(1)}, bf16[2,10,1024]{2,0,1:T(2,128)(2,1)S(1)}, u32[]{:S(2)}, u32[]{:S(2)}) collective-permute-start(bf16[2,10,1024]{2,0,1:T(2,128)(2,1)S(1)} %collective-permute-done.10), channel_id=1, source_target_pairs={{0,32},{32,64},{64,96},{96,128},{128,160},{160,192},{192,224},{224... | collective-permute-start | bytes 122888 | tf_op jit(solution)/shard_map/ppermute | solution.py:97
  356.5 9.3 %collective-permute-start.13 = (bf16[2,10,1024]{2,0,1:T(2,128)(2,1)S(1)}, bf16[2,10,1024]{2,0,1:T(2,128)(2,1)S(1)}, u32[]{:S(2)}, u32[]{:S(2)}) collective-permute-start(bf16[2,10,1024]{2,0,1:T(2,128)(2,1)S(1)} %collective-permute-done.11), channel_id=1, source_target_pairs={{0,480},{32,0},{64,32},{96,64},{128,96},{160,128},{192,160},{224,1... | collective-permute-start | bytes 122888 | tf_op jit(solution)/shard_map/ppermute | solution.py:102
  363.8 9.2 %collective-permute-start.14 = (bf16[2,10,1024]{2,0,1:T(2,128)(2,1)S(1)}, bf16[2,10,1024]{2,0,1:T(2,128)(2,1)S(1)}, u32[]{:S(2)}, u32[]{:S(2)}) collective-permute-start(bf16[2,10,1024]{2,0,1:T(2,128)(2,1)S(1)} %collective-permute-done.12), channel_id=1, source_target_pairs={{0,32},{32,64},{64,96},{96,128},{128,160},{160,192},{192,224},{224... | collective-permute-start | bytes 122888 | tf_op jit(solution)/shard_map/ppermute | solution.py:97
  375.7 1.3 copy-start.9
  375.8 119.5 %copy-start.6 = (bf16[16,2,1024]{2,1,0:T(2,128)(2,1)S(1)}, bf16[16,2,1024]{2,1,0:T(2,128)(2,1)}, u32[]{:S(2)}) copy-start(bf16[16,2,1024]{2,1,0:T(2,128)(2,1)} %param.12) | copy-start | bytes 196612
Sparse Core Ops, SparseCore 0:
  39.9 71.6 all-gather.4
  113.7 68.9 all-gather.2
  189.3 112.6 all-reduce.5
  377.1 117.0 all-reduce.7
